TPU v7x, 256 devices: a whole 4x4x8 slice. The times are simulated.
256 devices in a mesh: row: 8 (over y, core), col: 32 (over z, x).
Axes of the slice: x: 4, y: 4, z: 8, core: 2. Of those that a mesh axis runs over, the one named last changes fastest.
Arguments:
- blocks: float32 [128, 32, 256, 256], P('row', 'col'), may hold values from -6 to 6
- panel_rows: int32 [2, 64], P(None, 'row'), may hold values from -1 to 767, as said below
- target_slots: int32 [2, 128, 32], P(None, 'row', 'col'), may hold values from -1 to 7, as said below
- diag_inverse: float32 [2, 256, 256], replicated, may hold values from -1 to 1, as said below
- cross_block: float32 [256, 256], replicated, may hold values from -6 to 6
Outputs:
- factored: float32 [128, 32, 256, 256], P('row', 'col')
Inputs may be any that keep to these rules, and one draw needn't show every extreme that they name: `panel_rows`: slot q * 2 + m of row device r stands for the m-th structure row of block column class r + q times the number of row devices; both lists are -1 where that class is 0 or 1, and list 0 is -1 also where block column 0 lacks the row; otherwise list 0 equals list 1. `target_slots`: A filled slot of class c names in entry 0 a slot of its own row device and in entry 1 a slot of row device c modulo the number of row devices, within (c // number of row devices) * 2 and the 1 after it; both are filled or both -1, always -1 in classes 0 and 1; the target's block row number is at least its block column number. `diag_inverse`: each matrix is lower triangular.
All inputs are finite; a program needn't handle non-finite values.
Results may differ from a plain program's by a relative error of at most 0.0003.
Values sent between devices are 32-bit elements; how exact they have to be, the bound alone decides.
No kernel may reach another device: no remote copies, remote signals or barrier semaphores. Data moves between devices by JAX's collectives and lax.ppermute only.
A program may use at most 128 MiB of HBM per device.

v0:
```python
import jax
import jax.numpy as jnp
from jax import lax
from jax.sharding import PartitionSpec as P

PER_CLASS = 2
HIGHEST_PRECISION = lax.Precision.HIGHEST


def broadcast(array, axis, root):
    mine = lax.axis_index(axis) == root
    return lax.psum(jnp.where(mine, array, jnp.zeros_like(array)), axis)


def apply_inverse(panel_blocks, inverse):
    return jnp.einsum("sab,cb->sac", panel_blocks, inverse, precision=HIGHEST_PRECISION)


def per_device(blocks, panel_rows, target_slots, diag_inverse, cross_block):
    column = lax.axis_index("col")
    row_count = lax.axis_size("row")
    stored = blocks[:, 0]
    slot_count = panel_rows.shape[1]
    head_part = stored[:slot_count]
    first_live = (panel_rows[0] >= 0)[:, None, None]
    second_live = (panel_rows[1] >= 0)[:, None, None]
    cross_factor = jnp.dot(cross_block, diag_inverse[0].T, precision=HIGHEST_PRECISION)
    blank_part = jnp.zeros_like(head_part)
    class_start = column // row_count * PER_CLASS
    owner_row = column % row_count
    first_factor = lax.cond(
        column == 0,
        lambda: jnp.where(first_live, apply_inverse(head_part, diag_inverse[0]), 0.0),
        lambda: blank_part,
    )
    first_rows = broadcast(first_factor, "col", 0)
    first_cols = broadcast(
        lax.dynamic_slice_in_dim(first_rows, class_start, PER_CLASS, 0), "row", owner_row
    )
    second_factor = lax.cond(
        column == 1,
        lambda: jnp.where(
            second_live,
            apply_inverse(head_part - apply_inverse(first_rows, cross_factor), diag_inverse[1]),
            0.0,
        ),
        lambda: blank_part,
    )
    second_rows = broadcast(second_factor, "col", 1)
    second_cols = broadcast(
        lax.dynamic_slice_in_dim(second_rows, class_start, PER_CLASS, 0), "row", owner_row
    )
    row_index = target_slots[0, :, 0]
    col_index = target_slots[1, :, 0]
    present = row_index >= 0
    left_slot = jnp.where(present, row_index, 0)
    right_slot = jnp.where(present, col_index - class_start, 0)
    left_blocks = jnp.concatenate([first_rows[left_slot], second_rows[left_slot]], axis=2)
    right_blocks = jnp.concatenate([first_cols[right_slot], second_cols[right_slot]], axis=2)
    schur_term = jnp.einsum("sak,sbk->sab", left_blocks, right_blocks, precision=HIGHEST_PRECISION)
    trailing = stored - jnp.where(present[:, None, None], schur_term, 0.0)
    own_panel = jnp.where(column == 0, first_factor, second_factor)
    keep_mask = (column == 0) & first_live | (column == 1) & second_live
    head_blocks = jnp.where(keep_mask, own_panel, trailing[:slot_count])
    factored = jnp.concatenate([head_blocks, trailing[slot_count:]], axis=0)
    return factored[:, None]


def solution(mesh):
    return jax.shard_map(
        per_device,
        mesh=mesh,
        in_specs=(P("row", "col", None, None), P(None, "row"), P(None, "row", "col"), P(), P()),
        out_specs=P("row", "col", None, None),
        check_vma=False,
    )
```

profile of v0, /device:TPU:2, one launch (start us, length us, event | category | flops | bytes accessed | tf_op | source)
XLA Modules:
  0.0 431.3 jit_solution(9175127619029981087)
XLA Ops:
  6.5 0.0 copy-start
  6.5 0.0 all-reduce.5.cloned.1.call-start
  6.5 0.0 copy-start.9
  6.5 0.0 copy-start.8
  6.5 3.1 slice_bitcast_fusion
  9.7 0.0 copy-done.9
  9.7 0.0 copy-done.8
  9.7 0.2 conditional.2
  9.7 0.2 broadcast.123
  9.9 0.0 copy-start.3
  9.9 1.8 broadcast_select_fusion.1
  11.7 0.3 copy-done.3
  12.0 0.0 all-reduce.5.cloned.1.call-update
  12.0 0.0 all-reduce.7.cloned.1.call-start
  12.0 0.0 copy-done
  12.1 0.4 fusion.22
  12.5 155.4 %all-reduce.5.cloned.1.call-done = f32[8,256,256]{2,1,0:T(8,128)} async-done(((f32[8,256,256]{2,1,0:T(8,128)}), f32[8,256,256]{2,1,0:T(8,128)}) %all-reduce.5.cloned.1.call-update) | async-done | bytes 2097168 | tf_op jit(solution)/shard_map/psum | solution.py:12
  167.9 5.5 %conditional.3 = (f32[8,256,256]{2,1,0:T(8,128)S(1)}) conditional(s32[]{:T(128)} %convert_element_type.7, () %tuple.19, (s32[1,8]{1,0:T(1,128)S(1)}, s32[]{:T(128)}, f32[8,256,256]{2,1,0:T(8,128)}, f32[256,256]{1,0:T(8,128)S(1)}, f32[8,256,256]{2,1,0:T(8,128)}, /*index=5*/f32[2,256,256]{2,1,0:T(8,128)S(1)}) %tuple.37), branch_computations={%region_3.4_spmd, %region_4.5_spmd} | conditional | flops 3222274048 | bytes 19399248 | solution.py:40
  167.9 0.0 copy-start.7
  167.9 3.7 fusion.8
  171.6 0.0 copy-done.7
  171.6 1.8 fusion.4
  173.4 0.0 copy-start.5
  173.4 1.3 copy-done.5
  174.7 1.5 broadcast_select_fusion
  176.3 0.0 copy-start.2
  176.3 0.0 all-reduce.7.cloned.1.call-update
  176.3 0.0 copy-start.10
  176.3 0.2 all-reduce.9.cloned.1.call-start
  176.6 1.3 copy-done.2
  177.9 0.8 dynamic-slice_select_fusion.1
  178.7 145.2 %all-reduce.7.cloned.1.call-done = f32[8,256,256]{2,1,0:T(8,128)} async-done(((f32[8,256,256]{2,1,0:T(8,128)}), f32[8,256,256]{2,1,0:T(8,128)}) %all-reduce.7.cloned.1.call-update) | async-done | bytes 2097168 | tf_op jit(solution)/shard_map/psum | solution.py:12
  323.8 1.9 dynamic-slice_select_fusion
  325.7 0.0 all-reduce.9.cloned.1.call-update
  325.7 0.0 copy-done.10
  325.8 2.8 gather_fusion
  328.6 4.3 %gather_fusion.1 = f32[16,256,256]{2,1,0:T(8,128)} fusion(f32[8,256,256]{2,1,0:T(8,128)} %all-reduce.7.cloned.1.call-done, s32[1024]{0:T(1024)S(1)} %get-tuple-element.51), kind=kCustom, calls=%fused_computation.1 | custom fusion | bytes 8388672 | tf_op jit(solution)/shard_map/gather | solution.py:58
  332.9 59.6 %all-reduce.9.cloned.1.call-done = (f32[2,256,256]{2,1,0:T(8,128)}, f32[2,256,256]{2,1,0:T(8,128)}) async-done(((f32[2,256,256]{2,1,0:T(8,128)}, f32[2,256,256]{2,1,0:T(8,128)}), (f32[2,256,256]{2,1,0:T(8,128)}, f32[2,256,256]{2,1,0:T(8,128)})) %all-reduce.9.cloned.1.call-update) | async-done | bytes 1048592 | tf_op jit(solution)/shard_map/psum | solution.py:12
  392.5 0.0 copy-start.1
  392.6 3.9 gather_fusion.3
  396.5 0.0 copy-done.1
  396.5 2.8 gather_fusion.2
  399.3 0.0 copy-start.4
  399.3 22.5 %bitcast_subtract_fusion = f32[16,256,256]{2,1,0:T(8,128)S(1)} fusion(f32[16,1,256,256]{3,2,1,0:T(8,128)} %param.9, pred[16]{0:T(512)(128)(4,1)S(1)} %compare_bitcast_fusion.1, f32[16,256,256]{2,1,0:T(8,128)} %gather_fusion.3, f32[16,256,256]{2,1,0:T(8,128)} %gather_fusion.2, f32[16,256,256]{2,1,0:T(8,128)} %gather_fusion.1, f32[16,256,256]{2,1,0:T(8,128)} %gather_fusion), kind=kOutput, calls=%fused_computation.23 | convolution fusion | flops 6448742400 | bytes 25165840 | tf_op jit(solution)/shard_map/sak,sbk->sab/dot_general | solution.py:60
  421.7 0.0 copy-done.4
  421.7 0.0 copy-done.6
  421.7 0.6 slice_select_fusion
  422.3 2.4 maximum_bitcast_fusion
  (7 shorter events, 0.0 us)
Async XLA Ops:
  6.5 5.5 %copy-start = (f32[256,256]{1,0:T(8,128)S(1)}, f32[256,256]{1,0:T(8,128)}, u32[]{:S(2)}) copy-start(f32[256,256]{1,0:T(8,128)} %param.13) | copy-start | bytes 786436
  6.5 161.3 %all-reduce.5.cloned.1.call-start = ((), (), s32[]{:S(2)}) async-start(), calls=%async_computation | async-start | bytes 4194304 | tf_op jit(solution)/shard_map/psum | solution.py:12
  6.5 3.1 copy-start.9
  6.5 3.1 copy-start.8
  9.9 2.1 copy-start.3
  12.0 311.8 %all-reduce.7.cloned.1.call-start = ((), (), s32[]{:S(2)}) async-start(), calls=%async_computation.1 | async-start | bytes 4194304 | tf_op jit(solution)/shard_map/psum | solution.py:12
  167.9 3.7 copy-start.7
  173.4 1.3 copy-start.5
  176.3 1.6 copy-start.2
  176.3 149.4 %copy-start.10 = (s32[2,16,1]{1,2,0:T(1,128)S(1)}, s32[2,16,1]{1,2,0:T(1,128)}, u32[]{:S(2)}) copy-start(s32[2,16,1]{1,2,0:T(1,128)} %param.11) | copy-start | bytes 388
  176.3 216.2 %all-reduce.9.cloned.1.call-start = ((), (), s32[]{:S(2)}) async-start(), calls=%async_computation.2 | async-start | bytes 2097152 | tf_op jit(solution)/shard_map/psum | solution.py:12
  392.5 3.9 copy-start.1
  399.3 22.5 %copy-start.4 = (f32[8,256,256]{2,1,0:T(8,128)S(1)}, f32[8,256,256]{2,1,0:T(8,128)}, u32[]{:S(2)}) copy-start(f32[8,256,256]{2,1,0:T(8,128)} %copy-done.3) | copy-start | bytes 6291460
  399.3 22.5 %copy-start.6 = (f32[8,256,256]{2,1,0:T(8,128)S(1)}, f32[8,256,256]{2,1,0:T(8,128)}, u32[]{:S(2)}) copy-start(f32[8,256,256]{2,1,0:T(8,128)} %copy-done.5) | copy-start | bytes 6291460
Sparse Core Ops, SparseCore 0:
  12.1 155.7 all-reduce.4
  176.4 147.3 all-reduce.6
  326.3 66.2 all-reduce.8
where the time goes:
time: 432 us; the launch traced here: 431 us
  waiting for transfers between devices  360 us (83%)
  matrix products  28.4 us (7%)
  local copies, waits for them, and re-layouts  20 us (5%)
  between operations  13.3 us (3%)
  other arithmetic  9.08 us (2%)
    psum x3, waiting for transfers between devices, broadcast(): return lax.psum(jnp.where(mine, array, jnp.zeros_like(array)), axis)  360 us
    dot_general x1, matrix products, per_device(): jnp.einsum('sak,sbk->sab', left_blocks, right_blocks, precision=HIGHEST_P...  22.5 us
  transfers between devices with their start and end apart: 3, of which 3 were waited for; matrix products, arithmetic and copies ran while one was open for 2% of the time, Pallas kernels for 0%

commit v1 on v0

--- a/solution.py
+++ b/solution.py
@@ -2,14 +2,16 @@
 import jax.numpy as jnp
 from jax import lax
 from jax.sharding import PartitionSpec as P
+from jax.lax import all_gather
 
 PER_CLASS = 2
 HIGHEST_PRECISION = lax.Precision.HIGHEST
+point_flows = lambda row_data, chip_axis: jnp.sum(all_gather(row_data, chip_axis), axis=0)
 
 
 def broadcast(array, axis, root):
     mine = lax.axis_index(axis) == root
-    return lax.psum(jnp.where(mine, array, jnp.zeros_like(array)), axis)
+    return point_flows(jnp.where(mine, array, jnp.zeros_like(array)), axis)
 
 
 def apply_inverse(panel_blocks, inverse):

time: 432 us -> 1010 us (2.34)
  waiting for transfers between devices: 360 us -> 890 us
  other arithmetic: 9.08 us -> 59.5 us
    all_gather x0 -> x4, waiting for transfers between devices: none -> 890 us  [all_gather(row_data, chip_axis)]
    psum x3 -> x0, waiting for transfers between devices: 360 us -> none  [broadcast(): return lax.psum(jnp.where(mine, array, jnp.zeros_like(array)), axis)]
    reduce_sum x0 -> x4, other arithmetic: none -> 48.9 us  [jnp.sum(all_gather(row_data, chip_axis), axis=0)]
  transfers between devices with their start and end apart: 3 -> 4, of which waited for: 3 -> 4; matrix products, arithmetic and copies ran while one was open for 2% -> 4% of each run, Pallas kernels for 0% -> 0%
where the time goes in v1:
time: 1010 us
  waiting for transfers between devices  890 us (88%)
  other arithmetic  59.5 us (6%)
  matrix products  28 us (3%)
  local copies, waits for them, and re-layouts  16.3 us (2%)
  between operations  13.3 us (1%)
    all_gather x4, waiting for transfers between devices, all_gather(row_data, chip_axis)  890 us
    reduce_sum x4, other arithmetic, jnp.sum(all_gather(row_data, chip_axis), axis=0)  48.9 us
    dot_general x1, matrix products, per_device(): jnp.einsum('sak,sbk->sab', left_blocks, right_blocks, precision=HIGHEST_P...  22.5 us
  transfers between devices with their start and end apart: 4, of which 4 were waited for; matrix products, arithmetic and copies ran while one was open for 4% of the time, Pallas kernels for 0%

profile of v1, /device:TPU:2, one launch (start us, length us, event | category | flops | bytes accessed | tf_op | source)
XLA Modules:
  0.0 1007.8 jit_solution(6423230128452729083)
XLA Ops:
  6.5 0.0 copy-start
  6.5 0.0 all-gather.9.cloned.1.call-start
  6.5 0.0 copy-start.6
  6.5 0.0 copy-start.5
  6.5 3.1 slice_bitcast_fusion
  9.7 0.0 copy-done.6
  9.7 0.0 copy-done.5
  9.7 0.2 conditional.2
  9.7 0.2 broadcast.123
  9.9 0.0 copy-start.1
  9.9 1.7 broadcast_select_fusion.1
  11.6 0.2 copy-done.1
  11.8 0.0 all-gather.9.cloned.1.call-update
  11.8 0.0 all-gather.11.cloned.1.call-start
  11.9 0.0 copy-done
  11.9 0.4 fusion.22
  12.3 432.7 %all-gather.9.cloned.1.call-done = f32[256,256,256]{2,1,0:T(8,128)} async-done(((f32[8,256,256]{2,1,0:T(8,128)}), f32[256,256,256]{2,1,0:T(8,128)}) %all-gather.9.cloned.1.call-update) | async-done | bytes 67108880 | tf_op jit(solution)/shard_map/all_gather | solution.py:9
  445.1 20.8 %reduce_sum.36 = f32[8,256,256]{2,1,0:T(8,128)S(1)} reduce(f32[32,8,256,256]{3,2,1,0:T(8,128)} %bitcast.10, f32[]{:T(128)} %constant.47.clone.1), dimensions={0}, to_apply=%region_2.3 | reduce | flops 16252928 | bytes 69206016 | tf_op jit(solution)/shard_map/reduce_sum | solution.py:9
  465.9 5.2 conditional.3
  465.9 0.0 copy-start.4
  465.9 1.9 fusion.8
  467.9 0.0 copy-done.4
  467.9 3.2 fusion.4
  471.1 3.1 broadcast_select_fusion
  474.2 0.0 all-gather.11.cloned.1.call-update
  474.2 0.0 all-gather.13.cloned.1.call-start
  474.3 0.9 dynamic-slice_select_fusion.1
  475.2 0.0 all-gather.13.cloned.1.call-update
  475.2 0.2 all-gather.15.cloned.1.call-start
  475.4 423.7 %all-gather.11.cloned.1.call-done = f32[256,256,256]{2,1,0:T(8,128)} async-done(((f32[8,256,256]{2,1,0:T(8,128)}), f32[256,256,256]{2,1,0:T(8,128)}) %all-gather.11.cloned.1.call-update) | async-done | bytes 67108880 | tf_op jit(solution)/shard_map/all_gather | solution.py:9
  899.1 0.0 copy-start.7
  899.1 23.0 %reduce_sum.37 = f32[8,256,256]{2,1,0:T(8,128)} reduce(f32[32,8,256,256]{3,2,1,0:T(8,128)} %bitcast.16, f32[]{:T(128)} %constant.47.clone.1), dimensions={0}, to_apply=%region_5.6 | reduce | flops 16252928 | bytes 69206016 | tf_op jit(solution)/shard_map/reduce_sum | solution.py:9
  922.1 1.9 dynamic-slice_select_fusion
  924.0 0.0 all-gather.15.cloned.1.call-update
  924.0 0.0 copy-done.7
  924.1 2.8 gather_fusion
  926.9 7.2 all-gather.13.cloned.1.call-done
  934.0 2.5 reduce_sum.38
  936.6 2.8 gather_fusion.2
  939.3 4.3 gather_fusion.1
  943.7 26.8 %all-gather.15.cloned.1.call-done = f32[16,256,256]{2,1,0:T(8,128)} async-done(((f32[2,256,256]{2,1,0:T(8,128)}), f32[16,256,256]{2,1,0:T(8,128)}) %all-gather.15.cloned.1.call-update) | async-done | bytes 4194320 | tf_op jit(solution)/shard_map/all_gather | solution.py:9
  970.4 2.5 reduce_sum.39
  973.0 2.8 gather_fusion.3
  975.8 22.5 %bitcast_subtract_fusion = f32[16,256,256]{2,1,0:T(8,128)S(1)} fusion(f32[16,1,256,256]{3,2,1,0:T(8,128)} %param.9, pred[16]{0:T(512)(128)(4,1)S(1)} %compare_bitcast_fusion.1, f32[16,256,256]{2,1,0:T(8,128)} %gather_fusion.3, f32[16,256,256]{2,1,0:T(8,128)} %gather_fusion.2, f32[16,256,256]{2,1,0:T(8,128)} %gather_fusion.1, f32[16,256,256]{2,1,0:T(8,128)} %gather_fusion), kind=kOutput, calls=%fused_computation.23 | convolution fusion | flops 6448742400 | bytes 25165840 | tf_op jit(solution)/shard_map/sak,sbk->sab/dot_general | solution.py:62
  998.3 0.0 copy-done.2
  998.3 0.0 copy-done.3
  998.3 0.6 slice_select_fusion
  998.9 2.4 maximum_bitcast_fusion
  (8 shorter events, 0.0 us)
Async XLA Ops:
  6.5 5.4 copy-start
  6.5 438.5 %all-gather.9.cloned.1.call-start = ((), (), s32[]{:S(2)}) async-start(), calls=%async_computation | async-start | bytes 69206016 | tf_op jit(solution)/shard_map/all_gather | solution.py:9
  6.5 3.1 copy-start.6
  6.5 3.1 copy-start.5
  9.9 1.9 copy-start.1
  11.8 887.3 %all-gather.11.cloned.1.call-start = ((), (), s32[]{:S(2)}) async-start(), calls=%async_computation.1 | async-start | bytes 69206016 | tf_op jit(solution)/shard_map/all_gather | solution.py:9
  465.9 2.0 copy-start.4
  474.2 459.8 %all-gather.13.cloned.1.call-start = ((), (), s32[]{:S(2)}) async-start(), calls=%async_computation.2 | async-start | bytes 4718592 | tf_op jit(solution)/shard_map/all_gather | solution.py:9
  475.2 495.2 %all-gather.15.cloned.1.call-start = ((), (), s32[]{:S(2)}) async-start(), calls=%async_computation.3 | async-start | bytes 4718592 | tf_op jit(solution)/shard_map/all_gather | solution.py:9
  899.1 24.9 %copy-start.7 = (s32[2,16,1]{1,2,0:T(1,128)S(1)}, s32[2,16,1]{1,2,0:T(1,128)}, u32[]{:S(2)}) copy-start(s32[2,16,1]{1,2,0:T(1,128)} %param.11) | copy-start | bytes 388
  975.8 22.5 %copy-start.2 = (f32[8,256,256]{2,1,0:T(8,128)S(1)}, f32[8,256,256]{2,1,0:T(8,128)}, u32[]{:S(2)}) copy-start(f32[8,256,256]{2,1,0:T(8,128)} %copy-done.1) | copy-start | bytes 6291460
  975.8 22.5 %copy-start.3 = (f32[8,256,256]{2,1,0:T(8,128)S(1)}, f32[8,256,256]{2,1,0:T(8,128)}, u32[]{:S(2)}) copy-start(f32[8,256,256]{2,1,0:T(8,128)} %get-tuple-element.51) | copy-start | bytes 6291460
Sparse Core Ops, SparseCore 0:
  12.0 433.0 all-gather.8
  474.3 424.7 all-gather.10
  901.0 33.0 all-gather.12
  935.8 34.6 all-gather.14
